TPU v7x, 128 devices: a whole 4x4x4 slice. The times are simulated.
128 devices in a mesh: seq: 16 (over z, y), tp: 8 (over x, core).
Axes of the slice: x: 4, y: 4, z: 4, core: 2. Of those that a mesh axis runs over, the one named last changes fastest.
Arguments:
- hidden: bfloat16 [128, 64, 2560], P(None, 'seq'), may hold values from -6 to 6
- gain_attn: bfloat16 [2560], replicated, may hold values from 0.099609375 to 1.8984375
- w_query: bfloat16 [2560, 2560], P(None, 'tp'), may hold values from -0.125 to 0.125
- w_key: bfloat16 [2560, 640], P(None, 'tp'), may hold values from -0.375 to 0.375
- w_value: bfloat16 [2560, 640], P(None, 'tp'), may hold values from -0.25 to 0.25
- w_out: bfloat16 [2560, 2560], P('tp'), may hold values from -0.125 to 0.125
- gain_ffn: bfloat16 [2560], replicated, may hold values from 0.099609375 to 1.8984375
- w_gate: bfloat16 [2560, 6912], P(None, 'tp'), may hold values from -0.125 to 0.125
- w_up: bfloat16 [2560, 6912], P(None, 'tp'), may hold values from -0.125 to 0.125
- w_down: bfloat16 [6912, 2560], P('tp'), may hold values from -0.078125 to 0.078125
- shared_pages: bfloat16 [320, 8, 2, 80, 128], P('seq', 'tp'), may hold values from -270 to 270
- leaf_pages: bfloat16 [512, 8, 2, 80, 128], P('seq', 'tp'), may hold values from -270 to 270
- root_table: int32 [4, 16], replicated, may hold values from 0 to 319, as said below
- mid_table: int32 [16, 16], replicated, may hold values from 0 to 319, as said below
- leaf_table: int32 [64, 8], replicated, may hold values from 0 to 511, as said below
- root_len: int32 [4], replicated, may hold values from 1024 to 2048, as said below
- mid_len: int32 [16], replicated, may hold values from 1 to 2048, as said below
- leaf_len: int32 [64], replicated, may hold values from 1 to 1024, as said below
- mid_parent: int32 [16], replicated, may hold values from 0 to 3
- leaf_parent: int32 [64], replicated, may hold values from 0 to 15
- slot_request: int32 [64], replicated, may hold values from 0 to 63, as said below
Outputs:
- layer_out: float32 [128, 64, 2560], P('tp', 'seq')
Inputs may be any that keep to these rules, and one draw needn't show every extreme that they name: `slot_request`: A permutation of the requests. The 4 requests of slots 4 * s to 4 * s + 3 have their leaves with 4 distinct owners (see leaf_table). `leaf_table`: all pages of one request's leaf lie with one owner, the index of seq equal to page // 32; each owner holds the leaves of exactly 4 requests, and every leaf page is named once. `root_table`: with mid_table, names every shared page exactly once. Shared page g is held by the index of seq g // 20; each index holds exactly 1 page of every root. `mid_table`: with root_table, names every shared page exactly once. Each index of seq holds exactly 1 page of every middle node. `root_len`: some root reaches the largest value. `mid_len`: some middle node reaches the largest value. `leaf_len`: some leaf reaches the largest value.
All inputs are finite; a program needn't handle non-finite values.
Results may differ from a plain program's by a relative error of at most 0.009.
The roundings to bfloat16 on the way count: a program that leaves them out, or rounds other values in their place, can miss the bound.
Values may be sent and summed in bfloat16 or wider, within the bound.
No kernel may reach another device: no remote copies, remote signals or barrier semaphores. Data moves between devices by JAX's collectives and lax.ppermute only.
A program may use at most 192 MiB of HBM per device.

v0:
```python
import jax
import jax.numpy as jnp
from jax import lax
from jax.sharding import PartitionSpec as P

QH = 32
KVH = 8
HD = 80
WINDOW = 4096
masked_score = -1e30
rope_base = 10000.0


def rms_norm(row_data, gain_vector):
    values = row_data.astype(jnp.float32)
    inverse_rms = lax.rsqrt(jnp.mean(values * values, -1, keepdims=True) + 1e-05)
    return (values * inverse_rms * gain_vector.astype(jnp.float32)).astype(jnp.bfloat16)


def rotate(vector, position):
    half_size = vector.shape[-1] // 2
    frequency = rope_base ** (-2.0 * jnp.arange(half_size, dtype=jnp.float32) / vector.shape[-1])
    angles = position.astype(jnp.float32)[..., None] * frequency
    cos_part = jnp.cos(angles)
    sin_part = jnp.sin(angles)
    first_half = vector[..., :half_size]
    second_half = vector[..., half_size:]
    return jnp.concatenate(
        [
            first_half * cos_part - second_half * sin_part,
            second_half * cos_part + first_half * sin_part,
        ],
        -1,
    )


def page_columns(pages):
    moved = jnp.moveaxis(pages, -5, -2)
    return moved.reshape(moved.shape[:-2] + (moved.shape[-2] * moved.shape[-1],))


def attend(queries, key_pack, key_pos, present, query_pos):
    scores = jnp.einsum(
        "nbkge,bket->nbkgt", queries, key_pack[:, :, 0], preferred_element_type=jnp.float32
    ) * queries.shape[-1] ** (-0.5)
    distance = query_pos[:, :, None] - key_pos[None, :, :]
    allowed = (present[None, :, :] & (distance >= 0) & (distance < WINDOW))[:, :, None, None, :]
    scores = jnp.where(allowed, scores, masked_score)
    maximum = jnp.max(scores, -1)
    weights = jnp.where(allowed, jnp.exp(scores - maximum[..., None]), 0.0)
    totals = jnp.sum(weights, -1)
    weighted = jnp.einsum(
        "nbkgt,bket->nbkge",
        weights.astype(jnp.bfloat16),
        key_pack[:, :, 1],
        preferred_element_type=jnp.float32,
    )
    return (weighted, maximum, totals)


def merge_parts(first, second):
    maximum = jnp.maximum(first[1], second[1])
    first_scale = jnp.exp(first[1] - maximum)
    second_scale = jnp.exp(second[1] - maximum)
    return (
        first[0] * first_scale[..., None] + second[0] * second_scale[..., None],
        maximum,
        first[2] * first_scale + second[2] * second_scale,
    )


def spans(request_ids, root_len, mid_len, leaf_len, mid_parent, leaf_parent):
    mid_nodes = leaf_parent[request_ids]
    root_nodes = mid_parent[mid_nodes]
    return (root_nodes, mid_nodes, root_len[root_nodes], mid_len[mid_nodes], leaf_len[request_ids])


def shards(
    hidden,
    gain_attn,
    w_query,
    w_key,
    w_value,
    w_out,
    gain_ffn,
    w_gate,
    w_up,
    w_down,
    shared_pages,
    leaf_pages,
    root_table,
    mid_table,
    leaf_table,
    root_len,
    mid_len,
    leaf_len,
    mid_parent,
    leaf_parent,
    slot_request,
):
    new_rows, local_reqs, model_width = hidden.shape
    seq_count = lax.axis_size("seq")
    seq_index = lax.axis_index("seq")
    kv_local = leaf_pages.shape[1]
    group_size = QH // KVH
    pages_here = leaf_pages.shape[0]
    slot_ids = seq_index * local_reqs + jnp.arange(local_reqs, dtype=jnp.int32)
    requests = slot_request[slot_ids]
    root_nodes, mid_nodes, root_span, mid_span, leaf_span = spans(
        requests, root_len, mid_len, leaf_len, mid_parent, leaf_parent
    )
    context = root_span + mid_span + leaf_span
    new_index = jnp.arange(new_rows, dtype=jnp.int32)
    query_pos = context[None, :] + new_index[:, None]
    all_slots = slot_request.reshape(seq_count, local_reqs)
    page_store = lax.all_gather(shared_pages, "seq", axis=0, tiled=True)
    root_index = root_table[root_nodes]
    mid_index = mid_table[mid_nodes]
    normed = rms_norm(hidden, gain_attn).reshape(-1, model_width)
    query_proj = jnp.dot(normed, w_query, preferred_element_type=jnp.float32).reshape(
        new_rows, local_reqs, -1, HD
    )
    queries = (
        rotate(query_proj, query_pos[:, :, None])
        .astype(jnp.bfloat16)
        .reshape(new_rows, local_reqs, kv_local, group_size, HD)
    )
    key_proj = jnp.dot(normed, w_key, preferred_element_type=jnp.float32).reshape(
        new_rows, local_reqs, kv_local, HD
    )
    new_keys = rotate(key_proj, query_pos[:, :, None]).astype(jnp.bfloat16)
    new_values = (
        jnp.dot(normed, w_value, preferred_element_type=jnp.float32)
        .astype(jnp.bfloat16)
        .reshape(new_rows, local_reqs, kv_local, HD)
    )
    home_of = leaf_table[:, 0] // pages_here
    own_homes = home_of[requests]
    sender_match = home_of[all_slots] == seq_index
    sender_pick = jnp.argmax(sender_match, 1)
    sender_have = jnp.any(sender_match, 1)
    picked_request = jnp.take_along_axis(all_slots, sender_pick[:, None], 1)[:, 0]
    page_ids = jnp.where(
        sender_have[:, None], leaf_table[picked_request] - seq_index * pages_here, 0
    )
    leaf_steps = jnp.arange(leaf_table.shape[1] * leaf_pages.shape[-1], dtype=jnp.int32)
    fresh_pack = jnp.stack(
        [jnp.transpose(new_keys, (1, 2, 3, 0)), jnp.transpose(new_values, (1, 2, 3, 0))], 2
    )
    fresh_part = attend(
        queries,
        fresh_pack,
        context[:, None] + new_index[None, :],
        jnp.ones((local_reqs, new_rows), bool),
        query_pos,
    )
    outgoing = jnp.where(
        sender_have[:, None, None, None, None, None], jnp.take(leaf_pages, page_ids, axis=0), 0
    )
    arrived = lax.all_to_all(outgoing, "seq", split_axis=0, concat_axis=0, tiled=True)
    leaf_pack = page_columns(jnp.take(arrived, own_homes, axis=0))
    leaf_pos = (root_span + mid_span)[:, None] + leaf_steps[None, :]
    leaf_part = attend(
        queries, leaf_pack, leaf_pos, leaf_steps[None, :] < leaf_span[:, None], query_pos
    )
    root_pack = page_columns(jnp.take(page_store, root_index, axis=0))
    root_steps = jnp.arange(root_pack.shape[-1], dtype=jnp.int32)
    root_part = attend(
        queries,
        root_pack,
        root_steps[None, :] + 0 * root_span[:, None],
        root_steps[None, :] < root_span[:, None],
        query_pos,
    )
    mid_pack = page_columns(jnp.take(page_store, mid_index, axis=0))
    mid_steps = jnp.arange(mid_pack.shape[-1], dtype=jnp.int32)
    mid_part = attend(
        queries,
        mid_pack,
        root_span[:, None] + mid_steps[None, :],
        mid_steps[None, :] < mid_span[:, None],
        query_pos,
    )
    combined = merge_parts(merge_parts(root_part, mid_part), merge_parts(leaf_part, fresh_part))
    attended = (
        (combined[0] / combined[2][..., None])
        .astype(jnp.bfloat16)
        .reshape(new_rows * local_reqs, -1)
    )
    tp_count = lax.axis_size("tp")
    own_count = new_rows // tp_count
    attn_proj = lax.psum_scatter(
        jnp.dot(attended, w_out, preferred_element_type=jnp.float32),
        "tp",
        scatter_dimension=0,
        tiled=True,
    ).reshape(own_count, local_reqs, model_width)
    own_hidden = lax.dynamic_slice_in_dim(hidden, lax.axis_index("tp") * own_count, own_count, 0)
    resid = own_hidden.astype(jnp.float32) + attn_proj
    normed_own = rms_norm(resid, gain_ffn).reshape(-1, model_width)
    normed_ffn = lax.all_gather(normed_own, "tp", axis=0, tiled=True)
    gate_rows = jnp.dot(normed_ffn, w_gate, preferred_element_type=jnp.float32)
    up_rows = jnp.dot(normed_ffn, w_up, preferred_element_type=jnp.float32)
    activated = (jax.nn.silu(gate_rows) * up_rows).astype(jnp.bfloat16)
    ffn_proj = lax.psum_scatter(
        jnp.dot(activated, w_down, preferred_element_type=jnp.float32),
        "tp",
        scatter_dimension=0,
        tiled=True,
    ).reshape(own_count, local_reqs, model_width)
    return resid + ffn_proj


def solution(mesh):
    return jax.shard_map(
        shards,
        mesh=mesh,
        in_specs=(
            P(None, "seq", None),
            P(),
            P(None, "tp"),
            P(None, "tp"),
            P(None, "tp"),
            P("tp", None),
            P(),
            P(None, "tp"),
            P(None, "tp"),
            P("tp", None),
            P("seq", "tp", None, None, None),
            P("seq", "tp", None, None, None),
            P(),
            P(),
            P(),
            P(),
            P(),
            P(),
            P(),
            P(),
            P(),
        ),
        out_specs=P("tp", "seq", None),
        check_vma=False,
    )
```

profile of v0, /device:TPU:0, one launch (start us, length us, event | category | flops | bytes accessed | tf_op | source)
XLA Modules:
  0.0 381.0 jit_solution(9774462938295240041)
XLA Ops:
  6.5 0.7 all-gather.3.cloned.1.call-update
  7.3 0.7 reshape.786
  8.0 0.7 reshape.785
  8.8 0.8 copy.87
  9.6 0.7 and_select_fusion.1
  10.3 0.8 gather_fusion.9
  11.3 0.6 iota_reduce_fusion
  12.0 0.7 gather_fusion.13
  13.6 3.6 gather_fusion.11
  17.2 5.5 %select_select_fusion = bf16[16,8,1,2,80,128]{5,4,3,1,2,0:T(8,128)(2,1)} fusion(bf16[16,8,1,2,80,128]{5,4,3,1,2,0:T(8,128)(2,1)} %bitcast.319, pred[16]{0:T(512)(128)(4,1)S(1)} %reduce_or.9, pred[16,8]{1,0:T(8,128)(4,1)S(1)} %get-tuple-element.15), kind=kLoop, calls=%fused_computation.44 | loop fusion | flops 5242880 | bytes 10485904 | tf_op jit(solution)/shard_map/jit(_where)/select_n | solution.py:157
  22.7 8.3 %all-to-all-start = ((bf16[16,8,1,2,80,128]{5,4,3,1,2,0:T(8,128)(2,1)}), bf16[16,8,1,2,80,128]{5,4,3,1,2,0:T(8,128)(2,1)}, u32[]{:S(2)}, u32[]{:S(2)}) async-start(bf16[16,8,1,2,80,128]{5,4,3,1,2,0:T(8,128)(2,1)} %select_select_fusion), calls=%async_computation | async-start | bytes 10485760 | tf_op jit(solution)/shard_map/all_to_all | solution.py:160
  31.2 0.6 gather_fusion
  31.8 0.6 gather_fusion.8
  32.5 0.6 gather_fusion.6
  33.1 0.6 gather_fusion.1
  33.8 0.6 gather_fusion.5
  34.4 0.6 gather_fusion.2
  35.7 0.6 gather_fusion.4
  37.0 3.3 fusion.17
  40.4 3.0 fusion.19
  43.4 5.6 %reshape.793 = bf16[512,2560]{1,0:T(8,128)(2,1)} reshape(bf16[128,4,2560]{2,1,0:T(4,128)(2,1)} %fusion.19) | data formatting | bytes 5242880 | tf_op jit(solution)/shard_map/reshape | solution.py:119
  49.0 2.6 convolution_convert_fusion
  51.7 0.8 copy.93
  54.8 2.8 fusion.73
  57.6 1.5 fusion.136
  59.6 1.1 fusion.30
  60.9 0.6 copy-done.20
  62.1 0.6 compare_and_fusion.3
  64.0 1.4 fusion.37
  65.7 5.5 %fusion.26 = (pred[128,4,2048]{0,2,1:T(8,128)(4,1)}, pred[128,4,2048]{0,2,1:T(8,128)(4,1)}) fusion(s32[128,4]{0,1:T(4,128)S(1)} %get-tuple-element.27, pred[4,2048]{1,0:T(4,128)(4,1)S(1)} %iota_compare_fusion.1, s32[4,2048]{1,0:T(4,128)S(1)} %iota_add_fusion, pred[4,2048]{1,0:T(4,128)(4,1)S(1)} %iota_compare_fusion), kind=kLoop, calls=%fused_computation.51 | loop fusion | flops 10485760 | bytes 2148352 | tf_op jit(solution)/shard_map/and | solution.py:47
  71.2 56.7 %all-to-all-done = bf16[16,8,1,2,80,128]{5,4,3,1,2,0:T(8,128)(2,1)} async-done(((bf16[16,8,1,2,80,128]{5,4,3,1,2,0:T(8,128)(2,1)}), bf16[16,8,1,2,80,128]{5,4,3,1,2,0:T(8,128)(2,1)}, u32[]{:S(2)}, u32[]{:S(2)}) %all-to-all-start) | async-done | bytes 5242912 | tf_op jit(solution)/shard_map/all_to_all | solution.py:160
  127.9 3.4 gather_fusion.12
  131.3 0.8 fusion.41
  132.7 1.5 reshape.788
  134.1 2.5 fusion.14
  136.7 3.2 copy-done.10
  140.0 2.7 fusion.15
  142.7 15.5 %all-gather.3.cloned.1.call-done = bf16[320,1,2,80,128]{4,3,2,1,0:T(8,128)(2,1)} async-done(((bf16[20,1,2,80,128]{4,3,2,1,0:T(8,128)(2,1)}), bf16[320,1,2,80,128]{4,3,2,1,0:T(8,128)(2,1)}) %all-gather.3.cloned.1.call-update) | async-done | bytes 13107216 | tf_op jit(solution)/shard_map/all_gather | solution.py:116
  158.2 7.1 %gather_fusion.15 = bf16[64,2,80,128]{3,2,1,0:T(8,128)(2,1)} fusion(bf16[320,2,80,128]{3,2,1,0:T(8,128)(2,1)} %bitcast.325, s32[1024]{0:T(1024)S(1)} %copy-done.30), kind=kCustom, calls=%fused_computation.1.clone | custom fusion | bytes 5243136 | tf_op jit(solution)/shard_map/jit(_take)/gather | solution.py:175
  165.3 7.2 %gather_fusion.14 = bf16[64,2,80,128]{3,2,1,0:T(8,128)(2,1)} fusion(bf16[320,2,80,128]{3,2,1,0:T(8,128)(2,1)} %bitcast.326, s32[1024]{0:T(1024)S(1)} %copy-done.29), kind=kCustom, calls=%fused_computation.clone | custom fusion | bytes 5243136 | tf_op jit(solution)/shard_map/jit(_take)/gather | solution.py:166
  172.5 4.2 %fusion.35 = bf16[4,1,2,80,16,128]{5,4,3,0,2,1:T(8,128)(2,1)} fusion(bf16[4,16,1,2,80,128]{5,4,3,1,0,2:T(8,128)(2,1)} %bitcast.322, pred[4,16]{1,0:T(4,128)(4,1)S(1)} %copy-done.34), kind=kLoop, calls=%fused_computation.64 | loop fusion | flops 1310720 | bytes 5242944 | tf_op jit(solution)/shard_map/transpose | solution.py:38
  176.6 5.2 %reshape.777 = bf16[4,1,2,80,2048]{4,3,0,2,1:T(8,128)(2,1)} reshape(bf16[4,1,2,80,16,128]{5,4,3,0,2,1:T(8,128)(2,1)} %fusion.35) | data formatting | bytes 5242880 | tf_op jit(solution)/shard_map/reshape | solution.py:39
  181.8 4.3 %fusion.34 = bf16[4,1,2,80,16,128]{5,4,3,0,2,1:T(8,128)(2,1)} fusion(bf16[4,16,1,2,80,128]{5,4,3,1,0,2:T(8,128)(2,1)} %bitcast.321, pred[4,16]{1,0:T(4,128)(4,1)S(1)} %copy-done.33), kind=kLoop, calls=%fused_computation.62 | loop fusion | flops 1310720 | bytes 5242944 | tf_op jit(solution)/shard_map/transpose | solution.py:38
  186.1 5.2 %reshape.781 = bf16[4,1,2,80,2048]{4,3,0,2,1:T(8,128)(2,1)} reshape(bf16[4,1,2,80,16,128]{5,4,3,0,2,1:T(8,128)(2,1)} %fusion.34) | data formatting | bytes 5242880 | tf_op jit(solution)/shard_map/reshape | solution.py:39
  191.3 8.8 %fusion.1 = (f32[128,4,4]{0,2,1:T(4,128)S(1)}, f32[4,2048,128,4]{2,1,3,0:T(8,128)}) fusion(pred[128,4,2048]{0,2,1:T(8,128)(4,1)S(1)} %copy-done.12, bf16[128,4,4,40]{0,3,2,1:T(8,128)(2,1)S(1)} %copy-done.23, bf16[128,4,4,40]{0,3,2,1:T(8,128)(2,1)S(1)} %copy-done.21, bf16[4,1,2,80,2048]{4,3,0,2,1:T(8,128)(2,1)} %reshape.781), kind=kOutput, calls=%fused_computation.21 | convolution fusion | flops 684324864 | bytes 19472384 | tf_op jit(solution)/shard_map/nbkge,bket->nbkgt/dot_general | solution.py:43
  200.2 2.7 fusion
  203.0 10.7 %fusion.2 = (f32[128,4,4]{0,2,1:T(4,128)S(1)}, f32[128,4,4]{0,2,1:T(4,128)S(1)}) fusion(f32[4,2048,128,4]{2,1,3,0:T(8,128)S(1)} %get-tuple-element.36, f32[128,4,4]{0,2,1:T(4,128)S(1)} %get-tuple-element.35, pred[128,4,2048]{0,2,1:T(8,128)(4,1)S(1)} %copy-done.11, f32[128,4,4]{0,2,1:T(4,128)S(1)} %get-tuple-element.29, ...), kind=kLoop, calls=%fused_computation.22 | loop fusion | flops 41938944 | bytes 35684352 | tf_op jit(solution)/shard_map/reduce_sum | solution.py:51
  213.8 2.9 fusion.56
  216.7 10.7 %fusion.68 = f32[128,4,1,4,80]{0,4,3,1,2:T(8,128)} fusion(f32[4,2048,128,4]{2,1,3,0:T(8,128)} %get-tuple-element.30, f32[128,4,4]{0,2,1:T(4,128)S(1)} %get-tuple-element.29, pred[128,4,2048]{0,2,1:T(8,128)(4,1)S(1)} %copy-done.12, bf16[4,1,2,80,2048]{4,3,0,2,1:T(8,128)(2,1)} %reshape.781, f32[128,4,4]{0,2,1:T(4,128)S(1)} %bitcast.341), kind=kOutput, calls=%fused_computation.91 | convolution fusion | flops 692224000 | bytes 19808256 | tf_op jit(solution)/shard_map/nbkgt,bket->nbkge/dot_general | solution.py:52
  227.4 5.8 %fusion.65 = f32[128,4,1,4,80]{0,4,3,1,2:T(8,128)} fusion(f32[128,4,1,4,80]{0,4,3,1,2:T(8,128)} %fusion.68, f32[4,2048,128,4]{2,1,3,0:T(8,128)S(1)} %get-tuple-element.36, f32[128,4,4]{0,2,1:T(4,128)S(1)} %get-tuple-element.35, pred[128,4,2048]{0,2,1:T(8,128)(4,1)S(1)} %copy-done.11, bf16[4,1,2,80,2048]{4,3,0,2,1:T(8,128)(2,1)} %reshape.777, ...), kind=kOutput, calls=%fused_computation.90 | convolution fusion | flops 692551680 | bytes 20471808 | tf_op jit(solution)/shard_map/nbkgt,bket->nbkge/dot_general | solution.py:52
  233.2 1.7 fusion.72
  235.7 3.8 %fusion.124 = f32[512,2560]{1,0:T(8,128)} fusion(bf16[512,320]{1,0:T(8,128)(2,1)S(1)} %reshape.797, bf16[320,2560]{1,0:T(8,128)(2,1)S(1)} %copy-done), kind=kOutput, calls=%fused_computation.213 | convolution fusion | flops 838860800 | bytes 7208960 | tf_op jit(solution)/shard_map/dot_general | solution.py:193
  239.6 0.6 copy-done.32
  240.2 40.4 %reduce-scatter.3.cloned.1.call-done = f32[64,2560]{1,0:T(8,128)} async-done(((f32[512,2560]{1,0:T(8,128)}), f32[64,2560]{1,0:T(8,128)}) %reduce-scatter.3.cloned.1.call-update) | async-done | bytes 655376 | tf_op jit(solution)/shard_map/reduce_scatter | solution.py:192
  280.6 1.3 reshape.798
  281.9 1.3 multiply_reduce_fusion
  283.2 1.2 multiply_convert_fusion.1
  284.4 0.8 reshape.799
  285.5 25.5 %all-gather.5.cloned.1.call-done = bf16[512,2560]{1,0:T(8,128)(2,1)} async-done(((bf16[64,2560]{1,0:T(8,128)(2,1)}), bf16[512,2560]{1,0:T(8,128)(2,1)}) %all-gather.5.cloned.1.call-update) | async-done | bytes 2621456 | tf_op jit(solution)/shard_map/all_gather | solution.py:201
  311.0 6.8 %fusion.125 = f32[512,864]{0,1:T(8,128)} fusion(bf16[512,2560]{1,0:T(8,128)(2,1)} %all-gather.5.cloned.1.call-done, bf16[2560,864]{0,1:T(8,128)(2,1)} %param.30), kind=kOutput, calls=%fused_computation.214 | convolution fusion | flops 2264924160 | bytes 8814592 | tf_op jit(solution)/shard_map/dot_general | solution.py:202
  317.8 12.5 %fusion.78 = f32[512,2560]{1,0:T(8,128)} fusion(bf16[864,2560]{1,0:T(8,128)(2,1)} %param.32, f32[512,864]{0,1:T(8,128)} %fusion.125, bf16[512,2560]{1,0:T(8,128)(2,1)} %all-gather.5.cloned.1.call-done, bf16[2560,864]{0,1:T(8,128)(2,1)} %param.31), kind=kOutput, calls=%fused_computation.99 | convolution fusion | flops 4532502528 | bytes 18481152 | tf_op jit(solution)/shard_map/dot_general | solution.py:206
  330.3 40.6 %reduce-scatter.5.cloned.1.call-done = f32[64,2560]{1,0:T(8,128)} async-done(((f32[512,2560]{1,0:T(8,128)}), f32[64,2560]{1,0:T(8,128)}) %reduce-scatter.5.cloned.1.call-update) | async-done | bytes 655376 | tf_op jit(solution)/shard_map/reduce_scatter | solution.py:205
  371.0 1.3 reshape.800
  372.2 2.0 fusion.98
  (145 shorter events, 9.7 us)
Async XLA Ops:
  6.5 229.2 %copy-start = (bf16[320,2560]{1,0:T(8,128)(2,1)S(1)}, bf16[320,2560]{1,0:T(8,128)(2,1)}, u32[]{:S(2)}) copy-start(bf16[320,2560]{1,0:T(8,128)(2,1)} %param.28) | copy-start | bytes 4915204
  6.5 151.7 %all-gather.3.cloned.1.call-start = ((), (), s32[]{:S(2)}) async-start(), calls=%async_computation.3 | async-start | bytes 13926400 | tf_op jit(solution)/shard_map/all_gather | solution.py:116
  10.3 3.3 copy-start.9
  22.7 8.5 %copy-start.1 = (s32[64]{0:T(128)S(1)}, s32[64]{0:T(128)}, u32[]{:S(2)}) copy-start(s32[64]{0:T(128)} %param.43) | copy-start | bytes 772
  22.7 9.8 %copy-start.2 = (s32[64]{0:T(128)S(1)}, s32[64]{0:T(128)}, u32[]{:S(2)}) copy-start(s32[64]{0:T(128)} %param.40) | copy-start | bytes 772
  22.7 10.4 %copy-start.3 = (s32[64]{0:T(128)S(1)}, s32[64]{0:T(128)}, u32[]{:S(2)}) copy-start(s32[64]{0:T(128)} %param.42) | copy-start | bytes 772
  22.7 11.1 %copy-start.4 = (s32[16]{0:T(128)S(1)}, s32[16]{0:T(128)}, u32[]{:S(2)}) copy-start(s32[16]{0:T(128)} %param.39) | copy-start | bytes 196
  22.7 11.7 %copy-start.5 = (s32[16]{0:T(128)S(1)}, s32[16]{0:T(128)}, u32[]{:S(2)}) copy-start(s32[16]{0:T(128)} %param.41) | copy-start | bytes 196
  22.7 12.4 %copy-start.25 = (s32[16,16]{1,0:T(8,128)S(1)}, s32[16,16]{1,0:T(8,128)}, u32[]{:S(2)}) copy-start(s32[16,16]{1,0:T(8,128)} %param.36) | copy-start | bytes 3076
  22.7 13.0 %copy-start.6 = (s32[4]{0:T(128)S(1)}, s32[4]{0:T(128)}, u32[]{:S(2)}) copy-start(s32[4]{0:T(128)} %param.38) | copy-start | bytes 52
  22.7 13.7 %copy-start.24 = (s32[4,16]{1,0:T(4,128)S(1)}, s32[4,16]{1,0:T(4,128)}, u32[]{:S(2)}) copy-start(s32[4,16]{1,0:T(4,128)} %param.35) | copy-start | bytes 772
  22.7 14.3 %copy-start.31 = (bf16[2560]{0:T(1024)(128)(2,1)S(1)}, bf16[2560]{0:T(1024)(128)(2,1)}, u32[]{:S(2)}) copy-start(bf16[2560]{0:T(1024)(128)(2,1)} %param.24) | copy-start | bytes 15364
  22.7 105.2 %all-to-all-start = ((bf16[16,8,1,2,80,128]{5,4,3,1,2,0:T(8,128)(2,1)}), bf16[16,8,1,2,80,128]{5,4,3,1,2,0:T(8,128)(2,1)}, u32[]{:S(2)}, u32[]{:S(2)}) async-start(bf16[16,8,1,2,80,128]{5,4,3,1,2,0:T(8,128)(2,1)} %select_select_fusion), calls=%async_computation | async-start | bytes 10485760 | tf_op jit(solution)/shard_map/all_to_all | solution.py:160
  31.1 249.6 %reduce-scatter.3.cloned.1.call-start = ((), (), s32[]{:S(2)}) async-start(), calls=%async_computation.4 | async-start | bytes 5898240 | tf_op jit(solution)/shard_map/reduce_scatter | solution.py:192
  37.0 3.4 copy-start.7
  40.4 8.6 %copy-start.19 = (bf16[2560,80]{0,1:T(8,128)(2,1)S(1)}, bf16[2560,80]{0,1:T(8,128)(2,1)}, u32[]{:S(2)}) copy-start(bf16[2560,80]{0,1:T(8,128)(2,1)} %param.27) | copy-start | bytes 1228804
  43.4 11.3 %copy-start.36 = (bf16[2560,80]{0,1:T(8,128)(2,1)S(1)}, bf16[2560,80]{0,1:T(8,128)(2,1)}, u32[]{:S(2)}) copy-start(bf16[2560,80]{0,1:T(8,128)(2,1)} %param.26) | copy-start | bytes 1228804
  52.4 5.2 %copy-start.8 = (bf16[128,4,2560]{2,1,0:T(4,128)(2,1)S(1)}, bf16[128,4,2560]{2,1,0:T(4,128)(2,1)}, u32[]{:S(2)}) copy-start(bf16[128,4,2560]{2,1,0:T(4,128)(2,1)} %param.23) | copy-start | bytes 7864324
  54.8 4.9 %copy-start.35 = (bf16[2560,320]{0,1:T(8,128)(2,1)S(1)}, bf16[2560,320]{0,1:T(8,128)(2,1)}, u32[]{:S(2)}) copy-start(bf16[2560,320]{0,1:T(8,128)(2,1)} %param.25) | copy-start | bytes 4915204
  60.8 0.7 copy-start.20
  60.9 1.0 copy-start.22
  61.9 2.1 copy-start.17
  65.5 71.2 %copy-start.14 = (pred[128,4,1024]{0,2,1:T(8,128)(4,1)}, pred[128,4,1024]{0,2,1:T(8,128)(4,1)S(1)}, u32[]{:S(2)}) copy-start(pred[128,4,1024]{0,2,1:T(8,128)(4,1)S(1)} %fusion.37) | copy-start | bytes 1572868
  136.6 3.2 copy-start.10
  136.6 3.3 copy-start.26
  140.0 18.2 %copy-start.30 = (s32[1024]{0:T(1024)S(1)}, s32[1024]{0:T(1024)}, u32[]{:S(2)}) copy-start(s32[1024]{0:T(1024)} %pad_clamp_fusion.4) | copy-start | bytes 12292
  142.7 22.6 %copy-start.29 = (s32[1024]{0:T(1024)S(1)}, s32[1024]{0:T(1024)}, u32[]{:S(2)}) copy-start(s32[1024]{0:T(1024)} %pad_clamp_fusion.5) | copy-start | bytes 12292
  158.2 14.3 %copy-start.34 = (pred[4,16]{1,0:T(4,128)(4,1)S(1)}, pred[4,16]{1,0:T(4,128)(4,1)}, u32[]{:S(2)}) copy-start(pred[4,16]{1,0:T(4,128)(4,1)} %compare_and_fusion.2) | copy-start | bytes 196
  172.5 9.4 %copy-start.33 = (pred[4,16]{1,0:T(4,128)(4,1)S(1)}, pred[4,16]{1,0:T(4,128)(4,1)}, u32[]{:S(2)}) copy-start(pred[4,16]{1,0:T(4,128)(4,1)} %compare_and_fusion.1) | copy-start | bytes 196
  181.8 9.5 %copy-start.12 = (pred[128,4,2048]{0,2,1:T(8,128)(4,1)S(1)}, pred[128,4,2048]{0,2,1:T(8,128)(4,1)}, u32[]{:S(2)}) copy-start(pred[128,4,2048]{0,2,1:T(8,128)(4,1)} %get-tuple-element.26) | copy-start | bytes 3145732
  181.8 9.5 %copy-start.21 = (bf16[128,4,4,40]{0,3,2,1:T(8,128)(2,1)S(1)}, bf16[128,4,4,40]{0,3,2,1:T(8,128)(2,1)}, u32[]{:S(2)}) copy-start(bf16[128,4,4,40]{0,3,2,1:T(8,128)(2,1)} %copy-done.20) | copy-start | bytes 491524
  181.8 9.5 %copy-start.23 = (bf16[128,4,4,40]{0,3,2,1:T(8,128)(2,1)S(1)}, bf16[128,4,4,40]{0,3,2,1:T(8,128)(2,1)}, u32[]{:S(2)}) copy-start(bf16[128,4,4,40]{0,3,2,1:T(8,128)(2,1)} %copy-done.22) | copy-start | bytes 491524
  191.3 8.8 %copy-start.11 = (pred[128,4,2048]{0,2,1:T(8,128)(4,1)S(1)}, pred[128,4,2048]{0,2,1:T(8,128)(4,1)}, u32[]{:S(2)}) copy-start(pred[128,4,2048]{0,2,1:T(8,128)(4,1)} %get-tuple-element.25) | copy-start | bytes 3145732
  191.3 8.8 %copy-start.13 = (bf16[4,1,2,80,2048]{4,3,0,2,1:T(8,128)(2,1)S(1)}, bf16[4,1,2,80,2048]{4,3,0,2,1:T(8,128)(2,1)}, u32[]{:S(2)}) copy-start(bf16[4,1,2,80,2048]{4,3,0,2,1:T(8,128)(2,1)} %reshape.777) | copy-start | bytes 7864324
  200.2 13.6 %slice-start = ((s8[8388608]{0:T(1024)(128)(4,1)}), s8[4194304]{0:T(1024)(128)(4,1)S(1)}, s32[]{:S(2)}) async-start(s8[8388608]{0:T(1024)(128)(4,1)} %bitcast.323), calls=%async_computation.7 | async-start | bytes 8388608
  202.9 10.8 %copy-start.27 = (f32[128,4,4]{0,2,1:T(4,128)S(1)}, f32[128,4,4]{0,2,1:T(4,128)}, u32[]{:S(2)}) copy-start(f32[128,4,4]{0,2,1:T(4,128)} %copy-done.26) | copy-start | bytes 24580
  202.9 10.8 %copy-start.28 = (f32[128,4,4]{0,2,1:T(4,128)S(1)}, f32[128,4,4]{0,2,1:T(4,128)}, u32[]{:S(2)}) copy-start(f32[128,4,4]{0,2,1:T(4,128)} %fusion.15) | copy-start | bytes 24580
  202.9 10.8 %slice-start.1 = ((s8[8388608]{0:T(1024)(128)(4,1)}), s8[4194304]{0:T(1024)(128)(4,1)S(1)}, s32[]{:S(2)}) async-start(s8[8388608]{0:T(1024)(128)(4,1)} %bitcast.323), calls=%async_computation.8 | async-start | bytes 8388608
  202.9 10.8 %copy-start.15 = (pred[128,4,1024]{0,2,1:T(8,128)(4,1)S(1)}, pred[128,4,1024]{0,2,1:T(8,128)(4,1)}, u32[]{:S(2)}) copy-start(pred[128,4,1024]{0,2,1:T(8,128)(4,1)} %copy-done.14) | copy-start | bytes 1572868
  203.0 10.8 %copy-start.16 = (bf16[4,1,2,80,1024]{4,3,0,2,1:T(8,128)(2,1)S(1)}, bf16[4,1,2,80,1024]{4,3,0,2,1:T(8,128)(2,1)}, u32[]{:S(2)}) copy-start(bf16[4,1,2,80,1024]{4,3,0,2,1:T(8,128)(2,1)} %reshape.788) | copy-start | bytes 3932164
  227.4 5.8 %copy-start.18 = (f32[128,4,1,4,128]{0,4,3,1,2:T(8,128)S(1)}, f32[128,4,1,4,128]{0,4,3,1,2:T(8,128)}, u32[]{:S(2)}) copy-start(f32[128,4,1,4,128]{0,4,3,1,2:T(8,128)} %copy-done.17) | copy-start | bytes 3145732
  239.5 0.7 copy-start.32
  239.6 71.4 %all-gather.5.cloned.1.call-start = ((), (), s32[]{:S(2)}) async-start(), calls=%async_computation.5 | async-start | bytes 2949120 | tf_op jit(solution)/shard_map/all_gather | solution.py:201
  285.2 85.7 %reduce-scatter.5.cloned.1.call-start = ((), (), s32[]{:S(2)}) async-start(), calls=%async_computation.6 | async-start | bytes 5898240 | tf_op jit(solution)/shard_map/reduce_scatter | solution.py:205
Sparse Core Ops, SparseCore 0:
  9.5 148.6 all-gather.2
  239.7 40.9 reduce-scatter.2
  285.4 25.5 all-gather.4
  330.5 40.4 reduce-scatter.4
where the time goes:
time: 387 us; the launch traced here: 381 us
  waiting for transfers between devices  180 us (47%)
  matrix products  65.3 us (17%)
  local copies, waits for them, and re-layouts  59.2 us (15%)
  other arithmetic  54.4 us (14%)
  between operations  13.9 us (4%)
  starting transfers between devices  8.66 us (2%)
    all_to_all x1, waiting for transfers between devices, shards(): lax.all_to_all(outgoing, 'seq', split_axis=0, concat_axis=0, tiled=True)  56.7 us
    reduce_scatter x1, waiting for transfers between devices, shards(): lax.psum_scatter(jnp.dot(activated, w_down, preferred_element_type=jnp.fl...  40.6 us
    reduce_scatter x1, waiting for transfers between devices, shards(): lax.psum_scatter(jnp.dot(attended, w_out, preferred_element_type=jnp.floa...  40.4 us
    all_gather x1, waiting for transfers between devices, shards(): normed_ffn = lax.all_gather(normed_own, 'tp', axis=0, tiled=True)  25.5 us
    dot_general x4, matrix products, attend(): jnp.einsum('nbkgt,bket->nbkge', weights.astype(jnp.bfloat16), key_pack[:,...  21.1 us
    all_gather x1, waiting for transfers between devices, shards(): page_store = lax.all_gather(shared_pages, 'seq', axis=0, tiled=True)  15.5 us
    dot_general x4, matrix products, attend(): jnp.einsum('nbkge,bket->nbkgt', queries, key_pack[:, :, 0], preferred_ele...  14.4 us
    reduce_sum x3, other arithmetic, attend(): totals = jnp.sum(weights, -1)  13.6 us
  transfers between devices with their start and end apart: 5, of which 5 were waited for; matrix products, arithmetic and copies ran while one was open for 17% of the time, Pallas kernels for 0%

commit v1 on v0

--- a/solution.py
+++ b/solution.py
@@ -2,6 +2,7 @@
 import jax.numpy as jnp
 from jax import lax
 from jax.sharding import PartitionSpec as P
+from jax.lax import all_to_all, axis_size
 
 QH = 32
 KVH = 8
@@ -9,6 +10,9 @@
 WINDOW = 4096
 masked_score = -1e30
 rope_base = 10000.0
+time_shelves = lambda block_in: jnp.concatenate(
+    all_to_all(jnp.stack([block_in for _ in range(axis_size("seq"))]), "seq", 0, 0), axis=0
+)
 
 
 def rms_norm(row_data, gain_vector):
@@ -113,7 +117,7 @@
     new_index = jnp.arange(new_rows, dtype=jnp.int32)
     query_pos = context[None, :] + new_index[:, None]
     all_slots = slot_request.reshape(seq_count, local_reqs)
-    page_store = lax.all_gather(shared_pages, "seq", axis=0, tiled=True)
+    page_store = time_shelves(shared_pages)
     root_index = root_table[root_nodes]
     mid_index = mid_table[mid_nodes]
     normed = rms_norm(hidden, gain_attn).reshape(-1, model_width)

time: 387 us -> 542 us (1.40)
  waiting for transfers between devices: 180 us -> 320 us
  local copies, waits for them, and re-layouts: 59.2 us -> 71.7 us
  starting transfers between devices: 8.66 us -> 14.2 us
    all_to_all x0 -> x1, waiting for transfers between devices: none -> 136 us  [all_to_all(jnp.stack([block_in for _ in range(axis_size('seq'))]), 'seq',...]
    all_to_all x1, waiting for transfers between devices: 56.7 us -> 77.5 us  [shards(): lax.all_to_all(outgoing, 'seq', split_axis=0, concat_axis=0, tiled=True)]
    all_gather x1 -> x0, waiting for transfers between devices: 15.5 us -> none  [shards(): page_store = lax.all_gather(shared_pages, 'seq', axis=0, tiled=True)]
    another operation x0 -> x1, local copies, waits for them, and re-layouts: none -> 7.28 us  [jnp.stack([block_in for _ in range(axis_size('seq'))])]
    all_to_all x0 -> x1, starting transfers between devices: none -> 5.48 us  [all_to_all(jnp.stack([block_in for _ in range(axis_size('seq'))]), 'seq',...]
  transfers between devices with their start and end apart: 5 -> 5, of which waited for: 5 -> 5; matrix products, arithmetic and copies ran while one was open for 17% -> 9% of each run, Pallas kernels for 0% -> 0%
where the time goes in v1:
time: 542 us; the launch traced here: 535 us
  waiting for transfers between devices  320 us (59%)
  local copies, waits for them, and re-layouts  71.7 us (13%)
  matrix products  65.3 us (12%)
  other arithmetic  49.8 us (9%)
  starting transfers between devices  14.2 us (3%)
  between operations  14.1 us (3%)
    all_to_all x1, waiting for transfers between devices, all_to_all(jnp.stack([block_in for _ in range(axis_size('seq'))]), 'seq',...  136 us
    all_to_all x1, waiting for transfers between devices, shards(): lax.all_to_all(outgoing, 'seq', split_axis=0, concat_axis=0, tiled=True)  77.5 us
    reduce_scatter x1, waiting for transfers between devices, shards(): lax.psum_scatter(jnp.dot(activated, w_down, preferred_element_type=jnp.fl...  40.6 us
    reduce_scatter x1, waiting for transfers between devices, shards(): lax.psum_scatter(jnp.dot(attended, w_out, preferred_element_type=jnp.floa...  40 us
    all_gather x1, waiting for transfers between devices, shards(): normed_ffn = lax.all_gather(normed_own, 'tp', axis=0, tiled=True)  25.4 us
    dot_general x4, matrix products, attend(): jnp.einsum('nbkgt,bket->nbkge', weights.astype(jnp.bfloat16), key_pack[:,...  21.1 us
    dot_general x4, matrix products, attend(): jnp.einsum('nbkge,bket->nbkgt', queries, key_pack[:, :, 0], preferred_ele...  14.4 us
    reduce_sum x3, other arithmetic, attend(): totals = jnp.sum(weights, -1)  13.6 us
  transfers between devices with their start and end apart: 5, of which 5 were waited for; matrix products, arithmetic and copies ran while one was open for 9% of the time, Pallas kernels for 0%

profile of v1, /device:TPU:0, one launch (start us, length us, event | category | flops | bytes accessed | tf_op | source)
XLA Modules:
  0.0 534.7 jit_solution(1668870124835671392)
XLA Ops:
  6.5 0.9 reshape.793
  7.4 0.7 reshape.792
  8.1 0.7 and_select_fusion.1
  8.8 0.8 copy.85
  9.7 0.8 gather_fusion.9
  10.6 0.6 iota_reduce_fusion
  11.4 0.7 gather_fusion.13
  13.0 3.6 gather_fusion.11
  16.6 5.5 %select_select_fusion = bf16[16,8,1,2,80,128]{5,4,3,1,2,0:T(8,128)(2,1)} fusion(bf16[16,8,1,2,80,128]{5,4,3,1,2,0:T(8,128)(2,1)} %bitcast.322, pred[16]{0:T(512)(128)(4,1)S(1)} %reduce_or.9, pred[16,8]{1,0:T(8,128)(4,1)S(1)} %get-tuple-element.15), kind=kLoop, calls=%fused_computation.44 | loop fusion | flops 5242880 | bytes 10485904 | tf_op jit(solution)/shard_map/jit(_where)/select_n | solution.py:161
  22.1 8.3 %all-to-all-start.1 = ((bf16[16,8,1,2,80,128]{5,4,3,1,2,0:T(8,128)(2,1)}), bf16[16,8,1,2,80,128]{5,4,3,1,2,0:T(8,128)(2,1)}, u32[]{:S(2)}, u32[]{:S(2)}) async-start(bf16[16,8,1,2,80,128]{5,4,3,1,2,0:T(8,128)(2,1)} %select_select_fusion), calls=%async_computation.1 | async-start | bytes 10485760 | tf_op jit(solution)/shard_map/all_to_all | solution.py:164
  30.5 0.6 gather_fusion
  31.1 77.5 %all-to-all-done.1 = bf16[16,8,1,2,80,128]{5,4,3,1,2,0:T(8,128)(2,1)} async-done(((bf16[16,8,1,2,80,128]{5,4,3,1,2,0:T(8,128)(2,1)}), bf16[16,8,1,2,80,128]{5,4,3,1,2,0:T(8,128)(2,1)}, u32[]{:S(2)}, u32[]{:S(2)}) %all-to-all-start.1) | async-done | bytes 5242912 | tf_op jit(solution)/shard_map/all_to_all | solution.py:164
  108.6 7.3 %stack.2 = bf16[16,20,1,2,80,128]{5,4,3,2,1,0:T(8,128)(2,1)} broadcast(bf16[20,2,80,128]{3,2,1,0:T(8,128)(2,1)S(1)} %bitcast.328), dimensions={1,3,4,5} | broadcast | bytes 13926400 | tf_op jit(solution)/shard_map/stack | solution.py:14
  116.0 5.5 %all-to-all-start = ((bf16[16,20,1,2,80,128]{5,4,3,2,1,0:T(8,128)(2,1)}), bf16[16,20,1,2,80,128]{5,4,3,2,1,0:T(8,128)(2,1)}, u32[]{:S(2)}, u32[]{:S(2)}) async-start(bf16[16,20,1,2,80,128]{5,4,3,2,1,0:T(8,128)(2,1)} %stack.2), calls=%async_computation | async-start | bytes 26214400 | tf_op jit(solution)/shard_map/all_to_all | solution.py:14
  121.5 0.6 gather_fusion.8
  122.2 0.6 gather_fusion.6
  122.8 0.6 gather_fusion.1
  123.5 0.6 gather_fusion.5
  124.1 0.6 gather_fusion.2
  125.4 0.6 gather_fusion.4
  126.8 3.3 fusion.17
  130.1 3.0 fusion.19
  133.1 5.8 %reshape.800 = bf16[512,2560]{1,0:T(8,128)(2,1)} reshape(bf16[128,4,2560]{2,1,0:T(4,128)(2,1)} %fusion.19) | data formatting | bytes 5242880 | tf_op jit(solution)/shard_map/reshape | solution.py:123
  138.9 2.6 convolution_convert_fusion
  141.6 0.8 copy.91
  144.8 2.8 fusion.71
  148.0 1.5 fusion.134
  149.5 1.1 fusion.30
  153.7 1.4 fusion.35
  155.4 5.5 %fusion.26 = (pred[128,4,2048]{0,2,1:T(8,128)(4,1)}, pred[128,4,2048]{0,2,1:T(8,128)(4,1)}) fusion(s32[128,4]{0,1:T(4,128)S(1)} %get-tuple-element.27, pred[4,2048]{1,0:T(4,128)(4,1)S(1)} %iota_compare_fusion.1, s32[4,2048]{1,0:T(4,128)S(1)} %iota_add_fusion, pred[4,2048]{1,0:T(4,128)(4,1)S(1)} %iota_compare_fusion), kind=kLoop, calls=%fused_computation.51 | loop fusion | flops 10485760 | bytes 2148352 | tf_op jit(solution)/shard_map/and | solution.py:51
  160.9 3.4 gather_fusion.12
  164.3 0.8 fusion.39
  165.6 1.4 reshape.795
  167.1 2.5 fusion.14
  169.6 3.2 copy-done.10
  172.9 2.7 fusion.15
  175.6 136.0 %all-to-all-done = bf16[16,20,1,2,80,128]{5,4,3,2,1,0:T(8,128)(2,1)} async-done(((bf16[16,20,1,2,80,128]{5,4,3,2,1,0:T(8,128)(2,1)}), bf16[16,20,1,2,80,128]{5,4,3,2,1,0:T(8,128)(2,1)}, u32[]{:S(2)}, u32[]{:S(2)}) %all-to-all-start) | async-done | bytes 13107232 | tf_op jit(solution)/shard_map/all_to_all | solution.py:14
  311.6 7.1 %gather_fusion.15 = bf16[64,2,80,128]{3,2,1,0:T(8,128)(2,1)} fusion(bf16[320,2,80,128]{3,2,1,0:T(8,128)(2,1)} %bitcast.9, s32[1024]{0:T(1024)S(1)} %copy-done.31), kind=kCustom, calls=%fused_computation.1.clone | custom fusion | bytes 5243136 | tf_op jit(solution)/shard_map/jit(_take)/gather | solution.py:179
  318.7 7.1 %gather_fusion.14 = bf16[64,2,80,128]{3,2,1,0:T(8,128)(2,1)} fusion(bf16[320,2,80,128]{3,2,1,0:T(8,128)(2,1)} %bitcast.9, s32[1024]{0:T(1024)S(1)} %copy-done.30), kind=kCustom, calls=%fused_computation.clone | custom fusion | bytes 5243136 | tf_op jit(solution)/shard_map/jit(_take)/gather | solution.py:170
  325.8 2.0 select_bitcast_fusion.1
  327.8 2.5 copy.78
  330.4 5.2 reshape.784
  335.6 2.0 select_bitcast_fusion
  337.6 2.5 copy.83
  340.1 5.2 reshape.788
  345.3 8.8 %fusion.1 = (f32[128,4,4]{0,2,1:T(4,128)S(1)}, f32[4,2048,128,4]{2,1,3,0:T(8,128)}) fusion(pred[128,4,2048]{0,2,1:T(8,128)(4,1)S(1)} %copy-done.12, bf16[128,4,4,40]{0,3,2,1:T(8,128)(2,1)S(1)} %copy-done.24, bf16[128,4,4,40]{0,3,2,1:T(8,128)(2,1)S(1)} %copy-done.22, bf16[4,1,2,80,2048]{4,3,0,2,1:T(8,128)(2,1)} %reshape.788), kind=kOutput, calls=%fused_computation.21 | convolution fusion | flops 684324864 | bytes 19472384 | tf_op jit(solution)/shard_map/nbkge,bket->nbkgt/dot_general | solution.py:47
  354.2 2.7 fusion
  357.0 10.7 %fusion.2 = (f32[128,4,4]{0,2,1:T(4,128)S(1)}, f32[128,4,4]{0,2,1:T(4,128)S(1)}) fusion(f32[4,2048,128,4]{2,1,3,0:T(8,128)S(1)} %get-tuple-element.36, f32[128,4,4]{0,2,1:T(4,128)S(1)} %get-tuple-element.35, pred[128,4,2048]{0,2,1:T(8,128)(4,1)S(1)} %copy-done.11, f32[128,4,4]{0,2,1:T(4,128)S(1)} %get-tuple-element.29, ...), kind=kLoop, calls=%fused_computation.22 | loop fusion | flops 41938944 | bytes 35684352 | tf_op jit(solution)/shard_map/reduce_sum | solution.py:55
  367.8 3.0 fusion.54
  370.8 10.7 %fusion.66 = f32[128,4,1,4,80]{0,4,3,1,2:T(8,128)} fusion(f32[4,2048,128,4]{2,1,3,0:T(8,128)} %get-tuple-element.30, f32[128,4,4]{0,2,1:T(4,128)S(1)} %get-tuple-element.29, pred[128,4,2048]{0,2,1:T(8,128)(4,1)S(1)} %copy-done.12, bf16[4,1,2,80,2048]{4,3,0,2,1:T(8,128)(2,1)} %reshape.788, f32[128,4,4]{0,2,1:T(4,128)S(1)} %bitcast.343), kind=kOutput, calls=%fused_computation.89 | convolution fusion | flops 692224000 | bytes 19808256 | tf_op jit(solution)/shard_map/nbkgt,bket->nbkge/dot_general | solution.py:56
  381.4 5.8 %fusion.63 = f32[128,4,1,4,80]{0,4,3,1,2:T(8,128)} fusion(f32[128,4,1,4,80]{0,4,3,1,2:T(8,128)} %fusion.66, f32[4,2048,128,4]{2,1,3,0:T(8,128)S(1)} %get-tuple-element.36, f32[128,4,4]{0,2,1:T(4,128)S(1)} %get-tuple-element.35, pred[128,4,2048]{0,2,1:T(8,128)(4,1)S(1)} %copy-done.11, bf16[4,1,2,80,2048]{4,3,0,2,1:T(8,128)(2,1)} %reshape.784, ...), kind=kOutput, calls=%fused_computation.88 | convolution fusion | flops 692551680 | bytes 20471808 | tf_op jit(solution)/shard_map/nbkgt,bket->nbkge/dot_general | solution.py:56
  387.3 1.7 fusion.70
  389.7 3.8 fusion.122
  394.3 40.0 %reduce-scatter.3.cloned.1.call-done = f32[64,2560]{1,0:T(8,128)} async-done(((f32[512,2560]{1,0:T(8,128)}), f32[64,2560]{1,0:T(8,128)}) %reduce-scatter.3.cloned.1.call-update) | async-done | bytes 655376 | tf_op jit(solution)/shard_map/reduce_scatter | solution.py:196
  434.3 1.3 reshape.805
  435.6 1.3 multiply_reduce_fusion
  436.8 1.2 multiply_convert_fusion.1
  438.1 0.8 reshape.806
  439.2 25.4 %all-gather.2.cloned.1.call-done = bf16[512,2560]{1,0:T(8,128)(2,1)} async-done(((bf16[64,2560]{1,0:T(8,128)(2,1)}), bf16[512,2560]{1,0:T(8,128)(2,1)}) %all-gather.2.cloned.1.call-update) | async-done | bytes 2621456 | tf_op jit(solution)/shard_map/all_gather | solution.py:205
  464.6 6.8 %fusion.123 = f32[512,864]{0,1:T(8,128)} fusion(bf16[512,2560]{1,0:T(8,128)(2,1)} %all-gather.2.cloned.1.call-done, bf16[2560,864]{0,1:T(8,128)(2,1)} %param.30), kind=kOutput, calls=%fused_computation.212 | convolution fusion | flops 2264924160 | bytes 8814592 | tf_op jit(solution)/shard_map/dot_general | solution.py:206
  471.5 12.5 %fusion.76 = f32[512,2560]{1,0:T(8,128)} fusion(bf16[864,2560]{1,0:T(8,128)(2,1)} %param.32, f32[512,864]{0,1:T(8,128)} %fusion.123, bf16[512,2560]{1,0:T(8,128)(2,1)} %all-gather.2.cloned.1.call-done, bf16[2560,864]{0,1:T(8,128)(2,1)} %param.31), kind=kOutput, calls=%fused_computation.97 | convolution fusion | flops 4532502528 | bytes 18481152 | tf_op jit(solution)/shard_map/dot_general | solution.py:210
  484.0 40.6 %reduce-scatter.5.cloned.1.call-done = f32[64,2560]{1,0:T(8,128)} async-done(((f32[512,2560]{1,0:T(8,128)}), f32[64,2560]{1,0:T(8,128)}) %reduce-scatter.5.cloned.1.call-update) | async-done | bytes 655376 | tf_op jit(solution)/shard_map/reduce_scatter | solution.py:209
  524.6 1.3 reshape.807
  525.9 2.0 fusion.96
  (149 shorter events, 11.3 us)
Async XLA Ops:
  6.5 383.2 %copy-start = (bf16[320,2560]{1,0:T(8,128)(2,1)S(1)}, bf16[320,2560]{1,0:T(8,128)(2,1)}, u32[]{:S(2)}) copy-start(bf16[320,2560]{1,0:T(8,128)(2,1)} %param.28) | copy-start | bytes 4915204
  9.7 3.3 copy-start.9
  22.1 8.4 %copy-start.1 = (s32[64]{0:T(128)S(1)}, s32[64]{0:T(128)}, u32[]{:S(2)}) copy-start(s32[64]{0:T(128)} %param.43) | copy-start | bytes 772
  22.1 86.5 %copy-start.19 = (bf16[20,1,2,80,128]{4,3,2,1,0:T(8,128)(2,1)S(1)}, bf16[20,1,2,80,128]{4,3,2,1,0:T(8,128)(2,1)}, u32[]{:S(2)}) copy-start(bf16[20,1,2,80,128]{4,3,2,1,0:T(8,128)(2,1)} %param.33) | copy-start | bytes 2457604
  22.1 86.5 %all-to-all-start.1 = ((bf16[16,8,1,2,80,128]{5,4,3,1,2,0:T(8,128)(2,1)}), bf16[16,8,1,2,80,128]{5,4,3,1,2,0:T(8,128)(2,1)}, u32[]{:S(2)}, u32[]{:S(2)}) async-start(bf16[16,8,1,2,80,128]{5,4,3,1,2,0:T(8,128)(2,1)} %select_select_fusion), calls=%async_computation.1 | async-start | bytes 10485760 | tf_op jit(solution)/shard_map/all_to_all | solution.py:164
  115.9 6.3 %copy-start.2 = (s32[64]{0:T(128)S(1)}, s32[64]{0:T(128)}, u32[]{:S(2)}) copy-start(s32[64]{0:T(128)} %param.40) | copy-start | bytes 772
  115.9 6.9 %copy-start.3 = (s32[64]{0:T(128)S(1)}, s32[64]{0:T(128)}, u32[]{:S(2)}) copy-start(s32[64]{0:T(128)} %param.42) | copy-start | bytes 772
  115.9 7.6 %copy-start.4 = (s32[16]{0:T(128)S(1)}, s32[16]{0:T(128)}, u32[]{:S(2)}) copy-start(s32[16]{0:T(128)} %param.39) | copy-start | bytes 196
  115.9 8.2 %copy-start.5 = (s32[16]{0:T(128)S(1)}, s32[16]{0:T(128)}, u32[]{:S(2)}) copy-start(s32[16]{0:T(128)} %param.41) | copy-start | bytes 196
  115.9 8.8 %copy-start.26 = (s32[16,16]{1,0:T(8,128)S(1)}, s32[16,16]{1,0:T(8,128)}, u32[]{:S(2)}) copy-start(s32[16,16]{1,0:T(8,128)} %param.36) | copy-start | bytes 3076
  115.9 9.5 %copy-start.6 = (s32[4]{0:T(128)S(1)}, s32[4]{0:T(128)}, u32[]{:S(2)}) copy-start(s32[4]{0:T(128)} %param.38) | copy-start | bytes 52
  115.9 10.1 %copy-start.25 = (s32[4,16]{1,0:T(4,128)S(1)}, s32[4,16]{1,0:T(4,128)}, u32[]{:S(2)}) copy-start(s32[4,16]{1,0:T(4,128)} %param.35) | copy-start | bytes 772
  116.0 10.8 %copy-start.32 = (bf16[2560]{0:T(1024)(128)(2,1)S(1)}, bf16[2560]{0:T(1024)(128)(2,1)}, u32[]{:S(2)}) copy-start(bf16[2560]{0:T(1024)(128)(2,1)} %param.24) | copy-start | bytes 15364
  116.0 195.6 %all-to-all-start = ((bf16[16,20,1,2,80,128]{5,4,3,2,1,0:T(8,128)(2,1)}), bf16[16,20,1,2,80,128]{5,4,3,2,1,0:T(8,128)(2,1)}, u32[]{:S(2)}, u32[]{:S(2)}) async-start(bf16[16,20,1,2,80,128]{5,4,3,2,1,0:T(8,128)(2,1)} %stack.2), calls=%async_computation | async-start | bytes 26214400 | tf_op jit(solution)/shard_map/all_to_all | solution.py:14
  121.5 312.8 %reduce-scatter.3.cloned.1.call-start = ((), (), s32[]{:S(2)}) async-start(), calls=%async_computation.4 | async-start | bytes 5898240 | tf_op jit(solution)/shard_map/reduce_scatter | solution.py:196
  126.7 3.4 copy-start.7
  130.1 8.8 %copy-start.20 = (bf16[2560,80]{0,1:T(8,128)(2,1)S(1)}, bf16[2560,80]{0,1:T(8,128)(2,1)}, u32[]{:S(2)}) copy-start(bf16[2560,80]{0,1:T(8,128)(2,1)} %param.27) | copy-start | bytes 1228804
  133.1 11.7 %copy-start.37 = (bf16[2560,80]{0,1:T(8,128)(2,1)S(1)}, bf16[2560,80]{0,1:T(8,128)(2,1)}, u32[]{:S(2)}) copy-start(bf16[2560,80]{0,1:T(8,128)(2,1)} %param.26) | copy-start | bytes 1228804
  142.3 5.7 %copy-start.8 = (bf16[128,4,2560]{2,1,0:T(4,128)(2,1)S(1)}, bf16[128,4,2560]{2,1,0:T(4,128)(2,1)}, u32[]{:S(2)}) copy-start(bf16[128,4,2560]{2,1,0:T(4,128)(2,1)} %param.23) | copy-start | bytes 7864324
  144.8 4.7 copy-start.36
  150.7 0.7 copy-start.21
  150.7 1.0 copy-start.23
  151.8 1.9 copy-start.17
  155.2 14.5 %copy-start.14 = (pred[128,4,1024]{0,2,1:T(8,128)(4,1)}, pred[128,4,1024]{0,2,1:T(8,128)(4,1)S(1)}, u32[]{:S(2)}) copy-start(pred[128,4,1024]{0,2,1:T(8,128)(4,1)S(1)} %fusion.35) | copy-start | bytes 1572868
  169.6 3.3 copy-start.10
  169.6 3.3 copy-start.27
  172.9 138.7 %copy-start.31 = (s32[1024]{0:T(1024)S(1)}, s32[1024]{0:T(1024)}, u32[]{:S(2)}) copy-start(s32[1024]{0:T(1024)} %pad_clamp_fusion.4) | copy-start | bytes 12292
  175.5 143.1 %copy-start.30 = (s32[1024]{0:T(1024)S(1)}, s32[1024]{0:T(1024)}, u32[]{:S(2)}) copy-start(s32[1024]{0:T(1024)} %pad_clamp_fusion.5) | copy-start | bytes 12292
  311.6 14.2 %copy-start.35 = (pred[4,16]{1,0:T(4,128)(4,1)S(1)}, pred[4,16]{1,0:T(4,128)(4,1)}, u32[]{:S(2)}) copy-start(pred[4,16]{1,0:T(4,128)(4,1)} %compare_and_fusion.2) | copy-start | bytes 196
  327.8 7.7 %copy-start.34 = (pred[4,16]{1,0:T(4,128)(4,1)S(1)}, pred[4,16]{1,0:T(4,128)(4,1)}, u32[]{:S(2)}) copy-start(pred[4,16]{1,0:T(4,128)(4,1)} %compare_and_fusion.1) | copy-start | bytes 196
  337.6 7.7 %copy-start.12 = (pred[128,4,2048]{0,2,1:T(8,128)(4,1)S(1)}, pred[128,4,2048]{0,2,1:T(8,128)(4,1)}, u32[]{:S(2)}) copy-start(pred[128,4,2048]{0,2,1:T(8,128)(4,1)} %get-tuple-element.26) | copy-start | bytes 3145732
  337.6 7.7 %copy-start.22 = (bf16[128,4,4,40]{0,3,2,1:T(8,128)(2,1)S(1)}, bf16[128,4,4,40]{0,3,2,1:T(8,128)(2,1)}, u32[]{:S(2)}) copy-start(bf16[128,4,4,40]{0,3,2,1:T(8,128)(2,1)} %copy-done.21) | copy-start | bytes 491524
  337.6 7.7 %copy-start.24 = (bf16[128,4,4,40]{0,3,2,1:T(8,128)(2,1)S(1)}, bf16[128,4,4,40]{0,3,2,1:T(8,128)(2,1)}, u32[]{:S(2)}) copy-start(bf16[128,4,4,40]{0,3,2,1:T(8,128)(2,1)} %copy-done.23) | copy-start | bytes 491524
  345.3 8.8 %copy-start.11 = (pred[128,4,2048]{0,2,1:T(8,128)(4,1)S(1)}, pred[128,4,2048]{0,2,1:T(8,128)(4,1)}, u32[]{:S(2)}) copy-start(pred[128,4,2048]{0,2,1:T(8,128)(4,1)} %get-tuple-element.25) | copy-start | bytes 3145732
  345.3 8.8 %copy-start.13 = (bf16[4,1,2,80,2048]{4,3,0,2,1:T(8,128)(2,1)S(1)}, bf16[4,1,2,80,2048]{4,3,0,2,1:T(8,128)(2,1)}, u32[]{:S(2)}) copy-start(bf16[4,1,2,80,2048]{4,3,0,2,1:T(8,128)(2,1)} %reshape.784) | copy-start | bytes 7864324
  354.1 13.6 %slice-start = ((s8[8388608]{0:T(1024)(128)(4,1)}), s8[4194304]{0:T(1024)(128)(4,1)S(1)}, s32[]{:S(2)}) async-start(s8[8388608]{0:T(1024)(128)(4,1)} %bitcast.326), calls=%async_computation.7 | async-start | bytes 8388608
  356.9 10.8 %copy-start.28 = (f32[128,4,4]{0,2,1:T(4,128)S(1)}, f32[128,4,4]{0,2,1:T(4,128)}, u32[]{:S(2)}) copy-start(f32[128,4,4]{0,2,1:T(4,128)} %copy-done.27) | copy-start | bytes 24580
  356.9 10.8 %copy-start.29 = (f32[128,4,4]{0,2,1:T(4,128)S(1)}, f32[128,4,4]{0,2,1:T(4,128)}, u32[]{:S(2)}) copy-start(f32[128,4,4]{0,2,1:T(4,128)} %fusion.15) | copy-start | bytes 24580
  356.9 10.8 %slice-start.1 = ((s8[8388608]{0:T(1024)(128)(4,1)}), s8[4194304]{0:T(1024)(128)(4,1)S(1)}, s32[]{:S(2)}) async-start(s8[8388608]{0:T(1024)(128)(4,1)} %bitcast.326), calls=%async_computation.8 | async-start | bytes 8388608
  356.9 10.8 %copy-start.15 = (pred[128,4,1024]{0,2,1:T(8,128)(4,1)S(1)}, pred[128,4,1024]{0,2,1:T(8,128)(4,1)}, u32[]{:S(2)}) copy-start(pred[128,4,1024]{0,2,1:T(8,128)(4,1)} %copy-done.14) | copy-start | bytes 1572868
  356.9 10.8 %copy-start.16 = (bf16[4,1,2,80,1024]{4,3,0,2,1:T(8,128)(2,1)S(1)}, bf16[4,1,2,80,1024]{4,3,0,2,1:T(8,128)(2,1)}, u32[]{:S(2)}) copy-start(bf16[4,1,2,80,1024]{4,3,0,2,1:T(8,128)(2,1)} %reshape.795) | copy-start | bytes 3932164
  381.4 5.8 %copy-start.18 = (f32[128,4,1,4,128]{0,4,3,1,2:T(8,128)S(1)}, f32[128,4,1,4,128]{0,4,3,1,2:T(8,128)}, u32[]{:S(2)}) copy-start(f32[128,4,1,4,128]{0,4,3,1,2:T(8,128)} %copy-done.17) | copy-start | bytes 3145732
  393.6 0.7 copy-start.33
  393.6 71.0 %all-gather.2.cloned.1.call-start = ((), (), s32[]{:S(2)}) async-start(), calls=%async_computation.5 | async-start | bytes 2949120 | tf_op jit(solution)/shard_map/all_gather | solution.py:205
  438.9 85.7 %reduce-scatter.5.cloned.1.call-start = ((), (), s32[]{:S(2)}) async-start(), calls=%async_computation.6 | async-start | bytes 5898240 | tf_op jit(solution)/shard_map/reduce_scatter | solution.py:209
Sparse Core Ops, SparseCore 0:
  393.7 40.5 reduce-scatter.2
  439.0 25.5 all-gather.1
  484.1 40.4 reduce-scatter.4
